TPU v7x, 256 devices: a whole 4x4x8 slice. The times are simulated.
256 devices in a mesh: gx: 8 (over y, core), gy: 8 (over z), ba: 4 (over x).
Axes of the slice: x: 4, y: 4, z: 8, core: 2. Of those that a mesh axis runs over, the one named last changes fastest.
Arguments:
- pixels: float32 [224, 128, 1024], P('ba', 'gy', 'gx'), may hold values from -8 to 8
- spectra: float32 [224, 256], P('ba'), may hold values from -0.375 to 0.375
- abundance: float32 [256, 128, 1024], P('ba', 'gy', 'gx'), may hold values from 0 to 1
- plan: int32 [3], replicated, may hold values from 0 to 1, as said below
Outputs:
- sparse: float32 [256, 128, 1024], P('ba', 'gy', 'gx')
- spectra_grad: float32 [224, 256], P('ba')
Inputs may be any that keep to these rules, and one draw needn't show every extreme that they name: `plan`: entry 0 is 1 and at least one later entry is 0.
All inputs are finite; a program needn't handle non-finite values. Where the computation divides by a largest or mean magnitude, that divisor is 1e-20 or more.
Results may differ from a plain program's by a relative error of at most 0.0001.
Values sent between devices are 32-bit elements; how exact they have to be, the bound alone decides.
No kernel may reach another device: no remote copies, remote signals or barrier semaphores. Data moves between devices by JAX's collectives and lax.ppermute only.
A program may use at most 64 MiB of HBM per device.

v0:
```python
import math
import jax
import jax.numpy as jnp
from jax import lax
from jax.sharding import PartitionSpec as P

SWEEPS = 3
HIGHEST = lax.Precision.HIGHEST
penalty = 1.0
tv_weight = 0.2
sparsity = 0.05


def extended_2(x, sides, width):
    for axis, dim in sides:
        size, length = (lax.axis_size(axis), x.shape[dim])
        up = [(i, (i + 1) % size) for i in range(size - 1)]
        down = [(j, i) for i, j in up]
        last = lax.slice_in_dim(x, length - width, length, axis=dim)
        leading = lax.slice_in_dim(x, 0, width, axis=dim)
        before = lax.ppermute(last, axis, up)
        after = lax.ppermute(leading, axis, down)
        x = jnp.concatenate([before, x, after], axis=dim)
    return x


def edge_masks(top_row, left_col, row_count, col_count, grid_rows, grid_cols):
    ext_rows = top_row - 1 + jnp.arange(row_count + 1)
    ext_cols = left_col - 1 + jnp.arange(col_count + 1)
    rows_in = (ext_rows >= 0) & (ext_rows <= grid_rows - 1)
    cols_in = (ext_cols >= 0) & (ext_cols <= grid_cols - 1)
    rows_ok = (ext_rows >= 0) & (ext_rows <= grid_rows - 2)
    cols_ok = (ext_cols >= 0) & (ext_cols <= grid_cols - 2)
    mask_h = (rows_in[:, None] & cols_ok[None, :]).astype(jnp.float32)[None]
    mask_v = (rows_ok[:, None] & cols_in[None, :]).astype(jnp.float32)[None]
    return (mask_h, mask_v)


def local(pixels, spectra, abundance, plan):
    comp_share, row_count, gx_cols = abundance.shape
    band_ways = lax.axis_size("ba")
    grid_rows = row_count * lax.axis_size("gy")
    grid_cols = gx_cols * lax.axis_size("gx")
    all_comps = comp_share * band_ways
    top_row = lax.axis_index("gy") * row_count
    all_spectra = lax.all_gather(spectra, "ba", axis=0, tiled=True)
    first_comp = lax.axis_index("ba") * comp_share
    own_cols = lax.dynamic_slice_in_dim(all_spectra, first_comp, comp_share, 1)
    gram_rows = jnp.dot(own_cols.T, all_spectra, precision=HIGHEST)
    bound = lax.pmax(jnp.max(jnp.sum(jnp.abs(gram_rows), axis=1)), "ba")
    left_col = lax.axis_index("gx") * gx_cols
    mask_h, mask_v = edge_masks(top_row, left_col, row_count, gx_cols, grid_rows, grid_cols)
    field = abundance
    sparse = abundance
    dual = jnp.zeros_like(abundance)
    weight = jnp.ones((comp_share, row_count + 1, gx_cols + 1), jnp.float32)
    for sweep in range(SWEEPS):
        extended = extended_2(field, (("gx", 2), ("gy", 1)), 1)
        center = extended[:, : row_count + 1, : gx_cols + 1]
        right = extended[:, : row_count + 1, 1:]
        below = extended[:, 1:, : gx_cols + 1]
        diff_h = (right - center) * mask_h
        diff_v = (below - center) * mask_v
        energy = diff_h * diff_h + diff_v * diff_v
        total = lax.psum(jnp.sum(energy[:, 1:, 1:]), ("gx", "gy", "ba"))
        smooth_sq = total / (all_comps * grid_rows * grid_cols) + 1e-06
        fresh = 1.0 / jnp.sqrt(energy + smooth_sq)
        weight = jnp.where(plan[sweep] == 1, fresh, weight)
        flux_h = weight * diff_h
        flux_v = weight * diff_v
        edge_h = weight * mask_h
        edge_v = weight * mask_v
        tv_grad = flux_h[:, 1:, :-1] - flux_h[:, 1:, 1:] + flux_v[:, :-1, 1:] - flux_v[:, 1:, 1:]
        degree = edge_h[:, 1:, 1:] + edge_h[:, 1:, :-1] + edge_v[:, 1:, 1:] + edge_v[:, :-1, 1:]
        mixed = jnp.einsum(
            "lq,qrc->lrc",
            spectra,
            lax.all_gather(field, "ba", axis=0, tiled=True),
            precision=HIGHEST,
        )
        resid = mixed - pixels
        data_grad = lax.psum_scatter(
            jnp.einsum("lp,lrc->prc", spectra, resid, precision=HIGHEST),
            "ba",
            scatter_dimension=0,
            tiled=True,
        )
        grad_total = data_grad + tv_weight * tv_grad + penalty * (field - sparse + dual)
        field = field - grad_total / (bound + penalty + 2.0 * tv_weight * degree)
        sparse = jnp.maximum(field + dual - sparsity / penalty, 0.0)
        dual = dual + field - sparse
    all_sparse = lax.all_gather(sparse, "ba", axis=0, tiled=True)
    resid = jnp.einsum("lp,prc->lrc", spectra, all_sparse, precision=HIGHEST) - pixels
    partial_grad = jnp.einsum("lrc,prc->lp", resid, all_sparse, precision=HIGHEST) / math.sqrt(
        grid_rows * grid_cols
    )
    spectra_grad = lax.psum(partial_grad, ("gx", "gy"))
    return (sparse, spectra_grad)


def solution(mesh):
    return jax.shard_map(
        local,
        mesh=mesh,
        in_specs=(P("ba", "gy", "gx"), P("ba", None), P("ba", "gy", "gx"), P()),
        out_specs=(P("ba", "gy", "gx"), P("ba", None)),
        check_vma=False,
    )
```

profile of v0, /device:TPU:2, one launch (start us, length us, event | category | flops | bytes accessed | tf_op | source)
XLA Modules:
  0.0 793.5 jit_solution(9205692723680209742)
XLA Ops:
  7.2 0.7 all-gather.5.cloned.1.call-update
  8.0 37.2 %all-gather.5.cloned.1.call-done = f32[256,16,128]{2,1,0:T(8,128)} async-done(((f32[64,16,128]{2,1,0:T(8,128)}), f32[256,16,128]{2,1,0:T(8,128)}) %all-gather.5.cloned.1.call-update) | async-done | bytes 2097168 | tf_op jit(solution)/shard_map/all_gather | solution.py:78
  45.1 3.5 fusion.4
  48.8 1.8 convolution_bitcast_fusion.2
  50.6 2.0 copy.19
  52.7 1.0 copy-done.2
  53.9 1.6 collective-permute-start
  55.5 1.3 collective-permute-start.1
  56.8 12.2 %all_gather.16 = f32[224,256]{1,0:T(8,128)S(1)} all-gather(f32[56,256]{1,0:T(8,128)S(1)} %copy-done.14), channel_id=1, replica_groups=mesh['gx'=8,'gy'=8,'ba'=4] {'ba'}, dimensions={0}, use_global_device_ids=true | all-gather | bytes 286720 | tf_op jit(solution)/shard_map/all_gather | solution.py:46
  70.8 3.5 collective-permute-start.2
  74.2 0.7 fusion.73
  74.9 10.9 %pmax.7 = f32[]{:T(128)} all-reduce(f32[]{:T(128)} %reduce_max.9), channel_id=1, replica_groups=mesh['gx'=8,'gy'=8,'ba'=4] {'ba'}, use_global_device_ids=true, to_apply=%region_5.6 | all-reduce | flops 1 | bytes 8 | tf_op jit(solution)/shard_map/pmax | solution.py:50
  86.5 1.3 collective-permute-start.3
  87.8 0.7 maximum_maximum_fusion
  88.5 4.2 collective-permute-done.3
  92.6 0.9 multiply_add_fusion.2
  93.5 1.1 copy-done.3
  94.7 0.8 slice_reduce_fusion.2
  96.1 78.7 %psum.28 = f32[]{:T(128)} all-reduce(f32[]{:T(128)} %slice_reduce_fusion.2), channel_id=1, replica_groups=mesh['gx'=8,'gy'=8,'ba'=4] {'gx','gy','ba'}, use_global_device_ids=true, to_apply=%region_2.0 | all-reduce | flops 1 | bytes 8 | tf_op jit(solution)/shard_map/psum | solution.py:65
  175.5 5.1 fusion.55
  180.6 6.1 fusion.45
  187.0 30.1 %all-gather.7.cloned.1.call-done = f32[256,16,128]{2,1,0:T(8,128)} async-done(((f32[64,16,128]{2,1,0:T(8,128)}), f32[256,16,128]{2,1,0:T(8,128)}) %all-gather.7.cloned.1.call-update) | async-done | bytes 2097168 | tf_op jit(solution)/shard_map/all_gather | solution.py:78
  217.1 3.5 fusion.2
  220.8 1.8 convolution_bitcast_fusion.1
  222.6 2.0 copy.21
  224.7 1.0 copy-done
  225.8 1.6 collective-permute-start.4
  227.4 1.3 collective-permute-start.5
  228.9 3.7 collective-permute-done.5
  233.1 3.5 collective-permute-start.6
  236.6 1.3 collective-permute-start.7
  238.5 0.7 maximum_maximum_fusion.1
  239.2 3.6 collective-permute-done.7
  242.8 0.9 multiply_add_fusion.1
  243.7 1.2 copy-done.6
  244.8 0.8 slice_reduce_fusion.1
  246.3 83.2 %psum.29 = f32[]{:T(128)} all-reduce(f32[]{:T(128)} %slice_reduce_fusion.1), channel_id=1, replica_groups=mesh['gx'=8,'gy'=8,'ba'=4] {'gx','gy','ba'}, use_global_device_ids=true, to_apply=%region_8.9 | all-reduce | flops 1 | bytes 8 | tf_op jit(solution)/shard_map/psum | solution.py:65
  330.1 3.6 fusion.56
  333.8 1.1 copy-done.4
  334.9 2.7 fusion.68
  337.6 6.1 fusion.38
  344.0 29.8 %all-gather.9.cloned.1.call-done = f32[256,16,128]{2,1,0:T(8,128)} async-done(((f32[64,16,128]{2,1,0:T(8,128)}), f32[256,16,128]{2,1,0:T(8,128)}) %all-gather.9.cloned.1.call-update) | async-done | bytes 2097168 | tf_op jit(solution)/shard_map/all_gather | solution.py:78
  373.8 3.5 fusion
  377.5 1.8 convolution_bitcast_fusion
  379.3 2.0 copy.23
  381.4 1.0 copy-done.1
  382.5 1.6 collective-permute-start.8
  384.1 1.3 collective-permute-start.9
  385.6 3.7 collective-permute-done.9
  389.8 3.5 collective-permute-start.10
  393.3 1.3 collective-permute-start.11
  395.2 0.7 maximum_maximum_fusion.2
  395.9 3.6 collective-permute-done.11
  399.5 0.9 multiply_add_fusion
  400.4 1.2 copy-done.5
  401.5 0.8 slice_reduce_fusion
  403.0 83.4 %psum.30 = f32[]{:T(128)} all-reduce(f32[]{:T(128)} %slice_reduce_fusion), channel_id=1, replica_groups=mesh['gx'=8,'gy'=8,'ba'=4] {'gx','gy','ba'}, use_global_device_ids=true, to_apply=%region_11.12 | all-reduce | flops 1 | bytes 8 | tf_op jit(solution)/shard_map/psum | solution.py:65
  487.1 3.7 fusion.57
  490.8 2.6 fusion.69
  493.4 6.1 fusion.49
  499.6 30.1 %all-gather.11.cloned.1.call-done = f32[256,16,128]{2,1,0:T(8,128)} async-done(((f32[64,16,128]{2,1,0:T(8,128)}), f32[256,16,128]{2,1,0:T(8,128)}) %all-gather.11.cloned.1.call-update) | async-done | bytes 2097168 | tf_op jit(solution)/shard_map/all_gather | solution.py:92
  529.7 3.7 fusion.6
  533.5 2.3 fusion.22
  535.8 250.9 %psum.31 = f32[56,256]{1,0:T(8,128)} all-reduce(f32[56,256]{1,0:T(8,128)S(1)} %fusion.22), channel_id=1, replica_groups=mesh['gx'=8,'gy'=8,'ba'=4] {'gx','gy'}, use_global_device_ids=true, to_apply=%region_12.13 | all-reduce | flops 14336 | bytes 114688 | tf_op jit(solution)/shard_map/psum | solution.py:97
  (64 shorter events, 6.2 us)
Async XLA Ops:
  7.2 41.5 %copy-start.10 = (f32[56,16,128]{2,1,0:T(8,128)S(1)}, f32[56,16,128]{2,1,0:T(8,128)}, u32[]{:S(2)}) copy-start(f32[56,16,128]{2,1,0:T(8,128)} %param.4) | copy-start | bytes 1376260
  7.2 38.0 %all-gather.5.cloned.1.call-start = ((), (), s32[]{:S(2)}) async-start(), calls=%async_computation.3 | async-start | bytes 2621440 | tf_op jit(solution)/shard_map/all_gather | solution.py:78
  7.9 40.9 %copy-start.14 = (f32[56,256]{1,0:T(8,128)S(1)}, f32[56,256]{1,0:T(8,128)}, u32[]{:S(2)}) copy-start(f32[56,256]{1,0:T(8,128)} %param.5) | copy-start | bytes 172036
  7.9 172.7 %reduce-scatter.4.cloned.1.call-start = ((), (), s32[]{:S(2)}) async-start(), calls=%async_computation.4 | async-start | bytes 2621440 | tf_op jit(solution)/shard_map/reduce_scatter | solution.py:82
  52.6 1.0 copy-start.2
  52.6 164.5 %all-gather.7.cloned.1.call-start = ((), (), s32[]{:S(2)}) async-start(), calls=%async_computation.5 | async-start | bytes 2621440 | tf_op jit(solution)/shard_map/all_gather | solution.py:78
  53.9 20.4 %copy-start.15 = (s32[3]{0:T(128)S(1)}, s32[3]{0:T(128)}, u32[]{:S(2)}) copy-start(s32[3]{0:T(128)} %param.7) | copy-start | bytes 40
  53.9 16.4 %collective-permute-start = (f32[64,16,1]{2,1,0:T(8,128)S(1)}, f32[64,16,1]{2,1,0:T(8,128)S(1)}, u32[]{:S(2)}, u32[]{:S(2)}) collective-permute-start(f32[64,16,1]{2,1,0:T(8,128)S(1)} %get-tuple-element.28), channel_id=1, source_target_pairs={{0,32},{32,64},{64,96},{96,128},{128,160},{160,192},{192,224},{1,3... | collective-permute-start | bytes 12296 | tf_op jit(solution)/shard_map/ppermute | solution.py:21
  55.5 14.8 %collective-permute-start.1 = (f32[64,16,1]{2,1,0:T(8,128)S(1)}, f32[64,16,1]{2,1,0:T(8,128)S(1)}, u32[]{:S(2)}, u32[]{:S(2)}) collective-permute-start(f32[64,16,1]{2,1,0:T(8,128)S(1)} %get-tuple-element.29), channel_id=1, source_target_pairs={{32,0},{64,32},{96,64},{128,96},{160,128},{192,160},{224,192},{33,... | collective-permute-start | bytes 12296 | tf_op jit(solution)/shard_map/ppermute | solution.py:22
  70.8 17.0 %collective-permute-start.2 = (f32[64,1,130]{2,1,0:T(1,128)S(1)}, f32[64,1,130]{2,1,0:T(1,128)S(1)}, u32[]{:S(2)}, u32[]{:S(2)}) collective-permute-start(f32[64,1,130]{2,1,0:T(1,128)S(1)} %get-tuple-element.23), channel_id=1, source_target_pairs={{0,4},{4,8},{8,12},{12,16},{16,20},{20,24},{24,28},{1,5},{5,9},{9,... | collective-permute-start | bytes 99848 | tf_op jit(solution)/shard_map/ppermute | solution.py:21
  86.5 6.2 collective-permute-start.3
  93.5 1.1 copy-start.3
  186.7 33.9 %copy-start.11 = (f32[56,16,128]{2,1,0:T(8,128)S(1)}, f32[56,16,128]{2,1,0:T(8,128)}, u32[]{:S(2)}) copy-start(f32[56,16,128]{2,1,0:T(8,128)} %param.4) | copy-start | bytes 1376260
  186.7 150.9 %reduce-scatter.6.cloned.1.call-start = ((), (), s32[]{:S(2)}) async-start(), calls=%async_computation.6 | async-start | bytes 2621440 | tf_op jit(solution)/shard_map/reduce_scatter | solution.py:82
  224.6 1.0 copy-start
  224.6 149.2 %all-gather.9.cloned.1.call-start = ((), (), s32[]{:S(2)}) async-start(), calls=%async_computation.7 | async-start | bytes 2621440 | tf_op jit(solution)/shard_map/all_gather | solution.py:78
  225.8 3.1 collective-permute-start.4
  227.4 5.2 collective-permute-start.5
  233.1 5.3 collective-permute-start.6
  236.6 6.2 collective-permute-start.7
  243.7 1.2 copy-start.6
  333.8 1.1 copy-start.4
  343.7 33.6 %copy-start.12 = (f32[56,16,128]{2,1,0:T(8,128)S(1)}, f32[56,16,128]{2,1,0:T(8,128)}, u32[]{:S(2)}) copy-start(f32[56,16,128]{2,1,0:T(8,128)} %param.4) | copy-start | bytes 1376260
  343.7 149.7 %reduce-scatter.8.cloned.1.call-start = ((), (), s32[]{:S(2)}) async-start(), calls=%async_computation.8 | async-start | bytes 2621440 | tf_op jit(solution)/shard_map/reduce_scatter | solution.py:82
  381.3 1.0 copy-start.1
  381.3 148.3 %all-gather.11.cloned.1.call-start = ((), (), s32[]{:S(2)}) async-start(), calls=%async_computation.9 | async-start | bytes 2621440 | tf_op jit(solution)/shard_map/all_gather | solution.py:92
  382.5 3.1 collective-permute-start.8
  384.1 5.2 collective-permute-start.9
  389.3 10.1 %copy-start.7 = (f32[64,16,1]{2,1,0:T(8,128)}, f32[64,16,1]{2,1,0:T(8,128)S(1)}, u32[]{:S(2)}) copy-start(f32[64,16,1]{2,1,0:T(8,128)S(1)} %collective-permute-done.9) | copy-start | bytes 12292
  389.8 5.3 collective-permute-start.10
  393.3 6.2 collective-permute-start.11
  400.4 1.2 copy-start.5
  487.1 3.7 copy-start.8
  499.6 33.8 %copy-start.13 = (f32[56,16,128]{2,1,0:T(8,128)S(1)}, f32[56,16,128]{2,1,0:T(8,128)}, u32[]{:S(2)}) copy-start(f32[56,16,128]{2,1,0:T(8,128)} %param.4) | copy-start | bytes 1376260
  529.6 3.8 copy-start.9
Sparse Core Ops, SparseCore 0:
  9.8 35.2 all-gather.4
  52.8 32.7 reduce-scatter.3
  186.9 30.1 all-gather.6
  224.7 31.9 reduce-scatter.5
  343.9 29.8 all-gather.8
  381.4 31.9 reduce-scatter.7
  499.7 29.8 all-gather.10
where the time goes:
time: 795 us; the launch traced here: 794 us
  blocking collectives  519 us (65%)
  waiting for transfers between devices  148 us (19%)
  other arithmetic  46 us (6%)
  starting transfers between devices  23.6 us (3%)
  matrix products  22.7 us (3%)
  between operations  19.1 us (2%)
  local copies, waits for them, and re-layouts  14.7 us (2%)
    psum x1, blocking collectives, local(): spectra_grad = lax.psum(partial_grad, ('gx', 'gy'))  251 us
    psum x3, blocking collectives, local(): total = lax.psum(jnp.sum(energy[:, 1:, 1:]), ('gx', 'gy', 'ba'))  245 us
    all_gather x3, waiting for transfers between devices, local(): lax.all_gather(field, 'ba', axis=0, tiled=True)  97.1 us
    all_gather x1, waiting for transfers between devices, local(): all_sparse = lax.all_gather(sparse, 'ba', axis=0, tiled=True)  30.1 us
    ppermute x6, waiting for transfers between devices, extended_2(): after = lax.ppermute(leading, axis, down)  18.8 us
  transfers between devices with their start and end apart: 19, of which 13 were waited for; matrix products, arithmetic and copies ran while one was open for 4% of the time, Pallas kernels for 0%

commit v1 on v0

--- a/solution.py
+++ b/solution.py
@@ -94,7 +94,7 @@
     partial_grad = jnp.einsum("lrc,prc->lp", resid, all_sparse, precision=HIGHEST) / math.sqrt(
         grid_rows * grid_cols
     )
-    spectra_grad = lax.psum(partial_grad, ("gx", "gy"))
+    spectra_grad = jnp.sum(lax.all_gather(partial_grad, ("gx", "gy")), axis=0)
     return (sparse, spectra_grad)
 
 

time: 795 us -> 628 us (0.79)
  blocking collectives: 519 us -> 268 us
  waiting for transfers between devices: 148 us -> 228 us
    psum x1 -> x0, blocking collectives: 251 us -> none  [local(): spectra_grad = lax.psum(partial_grad, ('gx', 'gy'))]
    all_gather x0 -> x1, waiting for transfers between devices: none -> 79.7 us  [local(): spectra_grad = jnp.sum(lax.all_gather(partial_grad, ('gx', 'gy')), axis=0)]
  transfers between devices with their start and end apart: 19 -> 20, of which waited for: 13 -> 14; matrix products, arithmetic and copies ran while one was open for 4% -> 5% of each run, Pallas kernels for 0% -> 0%
where the time goes in v1:
time: 628 us; the launch traced here: 625 us
  blocking collectives  268 us (43%)
  waiting for transfers between devices  228 us (36%)
  other arithmetic  49 us (8%)
  starting transfers between devices  24 us (4%)
  matrix products  23.3 us (4%)
  between operations  18.9 us (3%)
  local copies, waits for them, and re-layouts  14.6 us (2%)
    psum x3, blocking collectives, local(): total = lax.psum(jnp.sum(energy[:, 1:, 1:]), ('gx', 'gy', 'ba'))  245 us
    all_gather x3, waiting for transfers between devices, local(): lax.all_gather(field, 'ba', axis=0, tiled=True)  97.1 us
    all_gather x1, waiting for transfers between devices, local(): spectra_grad = jnp.sum(lax.all_gather(partial_grad, ('gx', 'gy')), axis=0)  79.7 us
    all_gather x1, waiting for transfers between devices, local(): all_sparse = lax.all_gather(sparse, 'ba', axis=0, tiled=True)  29.8 us
    ppermute x6, waiting for transfers between devices, extended_2(): after = lax.ppermute(leading, axis, down)  18.8 us
    ppermute x6, starting transfers between devices, extended_2(): before = lax.ppermute(last, axis, up)  15.2 us
  transfers between devices with their start and end apart: 20, of which 14 were waited for; matrix products, arithmetic and copies ran while one was open for 5% of the time, Pallas kernels for 0%

profile of v1, /device:TPU:2, one launch (start us, length us, event | category | flops | bytes accessed | tf_op | source)
XLA Modules:
  0.0 625.5 jit_solution(1144763333941411932)
XLA Ops:
  7.2 0.7 all-gather.7.cloned.1.call-update
  8.0 37.2 %all-gather.7.cloned.1.call-done = f32[256,16,128]{2,1,0:T(8,128)} async-done(((f32[64,16,128]{2,1,0:T(8,128)}), f32[256,16,128]{2,1,0:T(8,128)}) %all-gather.7.cloned.1.call-update) | async-done | bytes 2097168 | tf_op jit(solution)/shard_map/all_gather | solution.py:78
  45.1 3.5 fusion.4
  48.8 1.8 convolution_bitcast_fusion.2
  50.6 1.9 copy.19
  52.7 1.0 copy-done.2
  53.8 1.6 collective-permute-start
  55.5 1.3 collective-permute-start.1
  56.8 12.2 %all_gather.22 = f32[224,256]{1,0:T(8,128)S(1)} all-gather(f32[56,256]{1,0:T(8,128)S(1)} %copy-done.14), channel_id=1, replica_groups=mesh['gx'=8,'gy'=8,'ba'=4] {'ba'}, dimensions={0}, use_global_device_ids=true | all-gather | bytes 286720 | tf_op jit(solution)/shard_map/all_gather | solution.py:46
  70.7 3.5 collective-permute-start.2
  74.8 10.9 %pmax.7 = f32[]{:T(128)} all-reduce(f32[]{:T(128)} %reduce_max.9), channel_id=1, replica_groups=mesh['gx'=8,'gy'=8,'ba'=4] {'ba'}, use_global_device_ids=true, to_apply=%region_5.6 | all-reduce | flops 1 | bytes 8 | tf_op jit(solution)/shard_map/pmax | solution.py:50
  86.4 1.3 collective-permute-start.3
  87.7 0.7 maximum_maximum_fusion
  88.4 4.2 collective-permute-done.3
  92.5 0.9 multiply_add_fusion.2
  93.4 1.1 copy-done.3
  94.6 0.8 slice_reduce_fusion.2
  96.0 78.7 %psum.21 = f32[]{:T(128)} all-reduce(f32[]{:T(128)} %slice_reduce_fusion.2), channel_id=1, replica_groups=mesh['gx'=8,'gy'=8,'ba'=4] {'gx','gy','ba'}, use_global_device_ids=true, to_apply=%region_2.0 | all-reduce | flops 1 | bytes 8 | tf_op jit(solution)/shard_map/psum | solution.py:65
  175.4 5.1 fusion.55
  180.5 6.2 fusion.45
  186.9 30.1 %all-gather.9.cloned.1.call-done = f32[256,16,128]{2,1,0:T(8,128)} async-done(((f32[64,16,128]{2,1,0:T(8,128)}), f32[256,16,128]{2,1,0:T(8,128)}) %all-gather.9.cloned.1.call-update) | async-done | bytes 2097168 | tf_op jit(solution)/shard_map/all_gather | solution.py:78
  217.0 3.5 fusion.2
  220.7 1.8 convolution_bitcast_fusion.1
  222.6 1.9 copy.21
  224.6 1.0 copy-done
  225.7 1.6 collective-permute-start.4
  227.4 1.3 collective-permute-start.5
  228.8 3.7 collective-permute-done.5
  233.0 3.5 collective-permute-start.6
  236.5 1.3 collective-permute-start.7
  238.4 0.7 maximum_maximum_fusion.1
  239.1 3.6 collective-permute-done.7
  242.7 0.9 multiply_add_fusion.1
  243.6 1.2 copy-done.6
  244.8 0.8 slice_reduce_fusion.1
  246.1 83.2 %psum.22 = f32[]{:T(128)} all-reduce(f32[]{:T(128)} %slice_reduce_fusion.1), channel_id=1, replica_groups=mesh['gx'=8,'gy'=8,'ba'=4] {'gx','gy','ba'}, use_global_device_ids=true, to_apply=%region_8.9 | all-reduce | flops 1 | bytes 8 | tf_op jit(solution)/shard_map/psum | solution.py:65
  329.9 3.6 fusion.56
  333.5 1.1 copy-done.4
  334.7 2.7 fusion.68
  337.4 6.2 fusion.38
  343.8 29.8 %all-gather.11.cloned.1.call-done = f32[256,16,128]{2,1,0:T(8,128)} async-done(((f32[64,16,128]{2,1,0:T(8,128)}), f32[256,16,128]{2,1,0:T(8,128)}) %all-gather.11.cloned.1.call-update) | async-done | bytes 2097168 | tf_op jit(solution)/shard_map/all_gather | solution.py:78
  373.6 3.5 fusion
  377.3 1.8 convolution_bitcast_fusion
  379.1 1.9 copy.23
  381.2 1.0 copy-done.1
  382.3 1.6 collective-permute-start.8
  384.0 1.3 collective-permute-start.9
  385.4 3.7 collective-permute-done.9
  389.6 3.5 collective-permute-start.10
  393.1 1.3 collective-permute-start.11
  395.0 0.7 maximum_maximum_fusion.2
  395.7 3.6 collective-permute-done.11
  399.3 0.9 multiply_add_fusion
  400.2 1.2 copy-done.5
  401.4 0.8 slice_reduce_fusion
  402.8 83.2 %psum.23 = f32[]{:T(128)} all-reduce(f32[]{:T(128)} %slice_reduce_fusion), channel_id=1, replica_groups=mesh['gx'=8,'gy'=8,'ba'=4] {'gx','gy','ba'}, use_global_device_ids=true, to_apply=%region_11.12 | all-reduce | flops 1 | bytes 8 | tf_op jit(solution)/shard_map/psum | solution.py:65
  486.6 3.7 fusion.57
  490.3 2.7 fusion.69
  493.0 6.1 fusion.49
  499.5 29.8 %all-gather.13.cloned.1.call-done = f32[256,16,128]{2,1,0:T(8,128)} async-done(((f32[64,16,128]{2,1,0:T(8,128)}), f32[256,16,128]{2,1,0:T(8,128)}) %all-gather.13.cloned.1.call-update) | async-done | bytes 2097168 | tf_op jit(solution)/shard_map/all_gather | solution.py:92
  529.2 3.7 fusion.6
  533.0 2.9 fusion.22
  536.0 79.7 %all-gather.15.cloned.1.call-done = f32[3584,256]{1,0:T(8,128)} async-done(((f32[56,256]{1,0:T(8,128)}), f32[3584,256]{1,0:T(8,128)}) %all-gather.15.cloned.1.call-update) | async-done | bytes 3670032 | tf_op jit(solution)/shard_map/all_gather | solution.py:97
  615.7 2.9 reduce_sum.49
  (67 shorter events, 7.1 us)
Async XLA Ops:
  7.2 41.5 %copy-start.10 = (f32[56,16,128]{2,1,0:T(8,128)S(1)}, f32[56,16,128]{2,1,0:T(8,128)}, u32[]{:S(2)}) copy-start(f32[56,16,128]{2,1,0:T(8,128)} %param.4) | copy-start | bytes 1376260
  7.2 38.0 %all-gather.7.cloned.1.call-start = ((), (), s32[]{:S(2)}) async-start(), calls=%async_computation.3 | async-start | bytes 2621440 | tf_op jit(solution)/shard_map/all_gather | solution.py:78
  7.9 40.9 %copy-start.14 = (f32[56,256]{1,0:T(8,128)S(1)}, f32[56,256]{1,0:T(8,128)}, u32[]{:S(2)}) copy-start(f32[56,256]{1,0:T(8,128)} %param.5) | copy-start | bytes 172036
  7.9 172.6 %reduce-scatter.4.cloned.1.call-start = ((), (), s32[]{:S(2)}) async-start(), calls=%async_computation.4 | async-start | bytes 2621440 | tf_op jit(solution)/shard_map/reduce_scatter | solution.py:82
  52.6 1.0 copy-start.2
  52.6 164.4 %all-gather.9.cloned.1.call-start = ((), (), s32[]{:S(2)}) async-start(), calls=%async_computation.5 | async-start | bytes 2621440 | tf_op jit(solution)/shard_map/all_gather | solution.py:78
  53.8 20.4 %copy-start.15 = (s32[3]{0:T(128)S(1)}, s32[3]{0:T(128)}, u32[]{:S(2)}) copy-start(s32[3]{0:T(128)} %param.7) | copy-start | bytes 40
  53.8 16.4 %collective-permute-start = (f32[64,16,1]{2,1,0:T(8,128)S(1)}, f32[64,16,1]{2,1,0:T(8,128)S(1)}, u32[]{:S(2)}, u32[]{:S(2)}) collective-permute-start(f32[64,16,1]{2,1,0:T(8,128)S(1)} %get-tuple-element.28), channel_id=1, source_target_pairs={{0,32},{32,64},{64,96},{96,128},{128,160},{160,192},{192,224},{1,3... | collective-permute-start | bytes 12296 | tf_op jit(solution)/shard_map/ppermute | solution.py:21
  55.5 14.8 %collective-permute-start.1 = (f32[64,16,1]{2,1,0:T(8,128)S(1)}, f32[64,16,1]{2,1,0:T(8,128)S(1)}, u32[]{:S(2)}, u32[]{:S(2)}) collective-permute-start(f32[64,16,1]{2,1,0:T(8,128)S(1)} %get-tuple-element.29), channel_id=1, source_target_pairs={{32,0},{64,32},{96,64},{128,96},{160,128},{192,160},{224,192},{33,... | collective-permute-start | bytes 12296 | tf_op jit(solution)/shard_map/ppermute | solution.py:22
  70.7 16.9 %collective-permute-start.2 = (f32[64,1,130]{2,1,0:T(1,128)S(1)}, f32[64,1,130]{2,1,0:T(1,128)S(1)}, u32[]{:S(2)}, u32[]{:S(2)}) collective-permute-start(f32[64,1,130]{2,1,0:T(1,128)S(1)} %get-tuple-element.23), channel_id=1, source_target_pairs={{0,4},{4,8},{8,12},{12,16},{16,20},{20,24},{24,28},{1,5},{5,9},{9,... | collective-permute-start | bytes 99848 | tf_op jit(solution)/shard_map/ppermute | solution.py:21
  86.4 6.2 collective-permute-start.3
  93.4 1.1 copy-start.3
  186.7 33.9 %copy-start.11 = (f32[56,16,128]{2,1,0:T(8,128)S(1)}, f32[56,16,128]{2,1,0:T(8,128)}, u32[]{:S(2)}) copy-start(f32[56,16,128]{2,1,0:T(8,128)} %param.4) | copy-start | bytes 1376260
  186.7 150.7 %reduce-scatter.6.cloned.1.call-start = ((), (), s32[]{:S(2)}) async-start(), calls=%async_computation.6 | async-start | bytes 2621440 | tf_op jit(solution)/shard_map/reduce_scatter | solution.py:82
  224.5 1.0 copy-start
  224.5 149.1 %all-gather.11.cloned.1.call-start = ((), (), s32[]{:S(2)}) async-start(), calls=%async_computation.7 | async-start | bytes 2621440 | tf_op jit(solution)/shard_map/all_gather | solution.py:78
  225.7 3.1 collective-permute-start.4
  227.4 5.2 collective-permute-start.5
  233.0 5.4 collective-permute-start.6
  236.5 6.2 collective-permute-start.7
  243.6 1.2 copy-start.6
  333.5 1.1 copy-start.4
  343.5 33.6 %copy-start.12 = (f32[56,16,128]{2,1,0:T(8,128)S(1)}, f32[56,16,128]{2,1,0:T(8,128)}, u32[]{:S(2)}) copy-start(f32[56,16,128]{2,1,0:T(8,128)} %param.4) | copy-start | bytes 1376260
  343.6 149.4 %reduce-scatter.8.cloned.1.call-start = ((), (), s32[]{:S(2)}) async-start(), calls=%async_computation.8 | async-start | bytes 2621440 | tf_op jit(solution)/shard_map/reduce_scatter | solution.py:82
  381.1 1.0 copy-start.1
  381.1 148.1 %all-gather.13.cloned.1.call-start = ((), (), s32[]{:S(2)}) async-start(), calls=%async_computation.9 | async-start | bytes 2621440 | tf_op jit(solution)/shard_map/all_gather | solution.py:92
  382.3 3.1 collective-permute-start.8
  384.0 5.2 collective-permute-start.9
  389.2 10.1 %copy-start.7 = (f32[64,16,1]{2,1,0:T(8,128)}, f32[64,16,1]{2,1,0:T(8,128)S(1)}, u32[]{:S(2)}) copy-start(f32[64,16,1]{2,1,0:T(8,128)S(1)} %collective-permute-done.9) | copy-start | bytes 12292
  389.6 5.4 collective-permute-start.10
  393.1 6.2 collective-permute-start.11
  400.2 1.2 copy-start.5
  486.6 3.7 copy-start.8
  499.1 33.8 %copy-start.13 = (f32[56,16,128]{2,1,0:T(8,128)S(1)}, f32[56,16,128]{2,1,0:T(8,128)}, u32[]{:S(2)}) copy-start(f32[56,16,128]{2,1,0:T(8,128)} %param.4) | copy-start | bytes 1376260
  499.2 116.6 %all-gather.15.cloned.1.call-start = ((), (), s32[]{:S(2)}) async-start(), calls=%async_computation.10 | async-start | bytes 3727360 | tf_op jit(solution)/shard_map/all_gather | solution.py:97
  529.2 3.8 copy-start.9
Sparse Core Ops, SparseCore 0:
  9.8 35.2 all-gather.6
  52.7 32.7 reduce-scatter.3
  186.8 30.1 all-gather.8
  224.6 32.0 reduce-scatter.5
  343.7 29.9 all-gather.10
  381.2 32.0 reduce-scatter.7
  499.3 29.8 all-gather.12
  536.1 79.5 all-gather.14
